TPU v7x, 256 devices: a whole 4x4x8 slice. The times are simulated.
256 devices in a mesh: sec: 2 (over y_lo), dp: 8 (over x, y_hi), seq: 16 (over z, core).
Axes of the slice: x: 4, y: 4 (y_hi: 2, y_lo: 2; y = y_hi * 2 + y_lo), z: 8, core: 2. Of those that a mesh axis runs over, the one named last changes fastest.
Arguments:
- hidden: bfloat16 [256, 128, 2560], P(('sec', 'dp', 'seq')), may hold values from -24 to 24
- cond_shift: bfloat16 [256, 2560], P(('sec', 'dp', 'seq')), may hold values from -0.3125 to 0.3125
- cond_scale: bfloat16 [256, 2560], P(('sec', 'dp', 'seq')), may hold values from -1.75 to 1.75
- noisy: bfloat16 [256, 128, 256], P(('sec', 'dp', 'seq')), may hold values from -6 to 6
- noise_level: float32 [256], P(('sec', 'dp', 'seq')), may hold values from 0.2 to 1
- w_out: bfloat16 [2560, 256], replicated, may hold values from -0.125 to 0.125
- w_embed: bfloat16 [256, 2048], replicated, may hold values from -0.375 to 0.375
- w_root: bfloat16 [2, 2048], replicated, may hold values from -0.03125 to 0.03125
- w_qkv: bfloat16 [3, 2048, 2048], P(None, None, 'seq'), may hold values from -0.125 to 0.125
- w_proj: bfloat16 [2048, 512], P('seq'), may hold values from -0.125 to 0.125
- text_table: bfloat16 [49408, 512], P('seq'), may hold values from -6 to 6
- text_ids: int32 [32, 32], replicated, may hold values from 0 to 49407
- prompt_index: int32 [256], P(('sec', 'dp')), may hold values from 0 to 31
- reward_weight: float32 [256], P(('sec', 'dp')), may hold values from 1000 to 4000
Outputs:
- rewards: float32 [256], P(('sec', 'dp'))
- grad_w_out: float32 [2560, 256], P('seq')
- grad_hidden: bfloat16 [256, 128, 2560], P(('sec', 'dp', 'seq'))
All inputs are finite; a program needn't handle non-finite values.
Results may differ from a plain program's by a relative error of at most 0.017.
The roundings to bfloat16 on the way count: a program that leaves them out, or rounds other values in their place, can miss the bound.
Values may be sent and summed in bfloat16 or wider, within the bound.
No kernel may reach another device: no remote copies, remote signals or barrier semaphores. Data moves between devices by JAX's collectives and lax.ppermute only.
A program may use at most 128 MiB of HBM per device.

v0:
```python
import jax
import jax.numpy as jnp
from jax import lax
from jax.sharding import PartitionSpec as P

D_REW = 2048
HEADS = 16
PROMPTS = 32
normalizing_sharpness = 10.0
epsilon = 1e-06
highest = lax.Precision.HIGHEST


def rotate(angle, first, second):
    cosine = jnp.cos(angle)
    sine_term = jnp.sin(angle)
    return (cosine * first + sine_term * second, cosine * second - sine_term * first)


def suffix(values):
    return jnp.sum(values, axis=1, keepdims=True) - jnp.cumsum(values, axis=1)


def local_path(motion):
    spin = motion[..., 0]
    theta = jnp.cumsum(spin, axis=1) - spin
    step_east, step_north = rotate(theta, motion[..., 1], motion[..., 2])
    path_east = jnp.cumsum(step_east, axis=1) - step_east
    path_north = jnp.cumsum(step_north, axis=1) - step_north
    return (theta, path_east, path_north)


def embed(motion, root_east, root_north, w_embed, root_rows):
    emb = jnp.einsum(
        "cfe,ed->cfd", motion.astype(jnp.bfloat16), w_embed, preferred_element_type=jnp.float32
    )
    emb = emb + root_east[..., None] * root_rows[0] + root_north[..., None] * root_rows[1]
    scale_rms = jnp.sqrt(jnp.mean(emb * emb, axis=-1, keepdims=True) + epsilon)
    return (emb / scale_rms, scale_rms)


def unit_rows(vectors):
    length = jnp.sqrt(jnp.sum(vectors * vectors, axis=-1, keepdims=True) + epsilon)
    return (vectors / length, length)


def norm_grad(grad, normed, scale_rms):
    return (grad - normed * jnp.mean(grad * normed, axis=-1, keepdims=True)) / scale_rms


def motion_grad(d_emb, normed_e, scale_rms, motion, theta, embed_rows, root_rows):
    d_unemb = norm_grad(d_emb, normed_e, scale_rms)
    d_embedded = jnp.einsum("cfd,ed->cfe", d_unemb, embed_rows, precision=highest)
    grad_east = suffix(jnp.sum(d_unemb * root_rows[0], axis=-1))
    grad_north = suffix(jnp.sum(d_unemb * root_rows[1], axis=-1))
    vel_east = motion[..., 1]
    vel_north = motion[..., 2]
    d_east, d_north = rotate(-theta, grad_east, grad_north)
    cosine = jnp.cos(theta)
    sine_term = jnp.sin(theta)
    d_theta = grad_east * (cosine * vel_north - sine_term * vel_east) - grad_north * (
        cosine * vel_east + sine_term * vel_north
    )
    d_spin = suffix(d_theta)
    return d_embedded.at[..., 0].add(d_spin).at[..., 1].add(d_east).at[..., 2].add(d_north)


def local(
    hidden,
    cond_shift,
    cond_scale,
    noisy,
    noise_level,
    w_out,
    w_embed,
    w_root,
    w_qkv,
    w_proj,
    text_table,
    text_ids,
    prompt_index,
    reward_weight,
):
    clips_dev = hidden.shape[0]
    ways = lax.axis_size("seq")
    group = clips_dev * ways
    frames = hidden.shape[1]
    width_cols = w_qkv.shape[2]
    head_size = D_REW // HEADS
    heads_dev = width_cols // head_size
    root_rows = w_root.astype(jnp.float32)
    embed_rows = w_embed.astype(jnp.float32)
    vocab_rows = text_table.shape[0]
    local_ids = text_ids - lax.axis_index("seq") * vocab_rows
    inside = (local_ids >= 0) & (local_ids < vocab_rows)
    picked = jnp.take(text_table, jnp.clip(local_ids, 0, vocab_rows - 1), axis=0).astype(
        jnp.float32
    )
    text_part = jnp.sum(jnp.where(inside[..., None], picked, 0.0), axis=1)
    text_raw = lax.psum(text_part, "seq")
    text_unit, text_len = unit_rows(text_raw)
    hidden_f = hidden.astype(jnp.float32)
    centred = hidden_f - jnp.mean(hidden_f, axis=-1, keepdims=True)
    inv_std = lax.rsqrt(jnp.mean(centred * centred, axis=-1, keepdims=True) + epsilon)
    normed_h = centred * inv_std
    gain = 1.0 + cond_scale.astype(jnp.float32)[:, None, :]
    modulated = (normed_h * gain + cond_shift.astype(jnp.float32)[:, None, :]).astype(jnp.bfloat16)
    eps_pred = jnp.einsum("cfd,de->cfe", modulated, w_out, preferred_element_type=jnp.float32)
    level = noise_level[:, None, None]
    x_clean = noisy.astype(jnp.float32) - level * eps_pred
    theta, path_east, path_north = local_path(x_clean)
    normed_e, scale_rms = embed(x_clean, path_east, path_north, w_embed, root_rows)
    projected = jnp.einsum(
        "cfd,jdk->cfjk",
        lax.all_gather(normed_e.astype(jnp.bfloat16), "seq", axis=0, tiled=True),
        w_qkv,
        preferred_element_type=jnp.float32,
    )
    projected = projected.reshape(group, frames, 3, heads_dev, head_size)
    query_unit, query_len = unit_rows(projected[:, :, 0])
    key_unit, key_len = unit_rows(projected[:, :, 1])
    asking_vectors_group = query_unit.astype(jnp.bfloat16)
    lookup_vectors_group = key_unit.astype(jnp.bfloat16)
    value_b = projected[:, :, 2].astype(jnp.bfloat16)
    similarity_table = normalizing_sharpness * jnp.einsum(
        "cfhd,cghd->chfg",
        asking_vectors_group,
        lookup_vectors_group,
        preferred_element_type=jnp.float32,
    )
    expo = jnp.exp(similarity_table)
    focus_probabilities = expo / jnp.sum(expo, axis=-1, keepdims=True)
    attention_b = focus_probabilities.astype(jnp.bfloat16)
    column_mass = jnp.sum(attention_b, axis=2, dtype=jnp.float32)
    value_f = value_b.astype(jnp.float32)
    pooled = jnp.einsum("chg,cghd->chd", column_mass, value_f, precision=highest)
    pooled_b = pooled.astype(jnp.bfloat16).reshape(group, width_cols)
    motion_part = jnp.dot(pooled_b, w_proj, preferred_element_type=jnp.float32)
    motion_emb = lax.psum(motion_part, "seq")
    choose = (prompt_index[:, None] == jnp.arange(PROMPTS)[None, :]).astype(jnp.float32)
    target = jnp.dot(choose, text_unit, precision=highest)
    emb_len = jnp.sqrt(jnp.sum(motion_emb * motion_emb, axis=-1) + epsilon)
    rewards = jnp.sum(motion_emb * target, axis=-1) / emb_len
    d_memb = (
        (-reward_weight)[:, None]
        * (target - rewards[:, None] * motion_emb / emb_len[:, None])
        / emb_len[:, None]
    )
    d_pooled = jnp.dot(d_memb, w_proj.astype(jnp.float32).T, precision=highest).reshape(
        group, heads_dev, head_size
    )
    reduction_dimension = jnp.einsum("chd,cghd->chg", d_pooled, value_f, precision=highest)
    d_value = jnp.transpose(column_mass, (0, 2, 1))[..., None] * d_pooled[:, None]
    pairwise_dot_similarity = jnp.sum(
        focus_probabilities * reduction_dimension[:, :, None, :], axis=-1, keepdims=True
    )
    similarity_derivative = (
        normalizing_sharpness
        * focus_probabilities
        * (reduction_dimension[:, :, None, :] - pairwise_dot_similarity)
    ).astype(jnp.bfloat16)
    d_qu = jnp.einsum(
        "chfg,cghd->cfhd",
        similarity_derivative,
        lookup_vectors_group,
        preferred_element_type=jnp.float32,
    )
    d_ku = jnp.einsum(
        "chfg,cfhd->cghd",
        similarity_derivative,
        asking_vectors_group,
        preferred_element_type=jnp.float32,
    )
    d_query = (d_qu - query_unit * jnp.sum(query_unit * d_qu, axis=-1, keepdims=True)) / query_len
    d_key = (d_ku - key_unit * jnp.sum(key_unit * d_ku, axis=-1, keepdims=True)) / key_len
    d_proj = (
        jnp.stack([d_query, d_key, d_value], axis=2)
        .astype(jnp.bfloat16)
        .reshape(group, frames, 3, width_cols)
    )
    d_emb = lax.psum_scatter(
        jnp.einsum("cfjk,jdk->cfd", d_proj, w_qkv, preferred_element_type=jnp.float32),
        "seq",
        scatter_dimension=0,
        tiled=True,
    )
    d_motion = motion_grad(d_emb, normed_e, scale_rms, x_clean, theta, embed_rows, root_rows)
    d_eps_b = (-level * d_motion).astype(jnp.bfloat16)
    d_mod = jnp.einsum("cfe,de->cfd", d_eps_b, w_out, preferred_element_type=jnp.float32)
    d_norm = d_mod * gain
    grad_hidden = (
        inv_std
        * (
            d_norm
            - jnp.mean(d_norm, axis=-1, keepdims=True)
            - normed_h * jnp.mean(d_norm * normed_h, axis=-1, keepdims=True)
        )
    ).astype(jnp.bfloat16)
    rows_dev = w_out.shape[0] // ways
    grad_term = jnp.einsum("cfd,cfe->de", modulated, d_eps_b, preferred_element_type=jnp.float32)
    grad_total = lax.psum(grad_term, ("sec", "dp", "seq"))
    grad_w_out = lax.dynamic_slice_in_dim(grad_total, lax.axis_index("seq") * rows_dev, rows_dev, 0)
    return (rewards, grad_w_out, grad_hidden)


def solution(mesh):
    placed = (
        P(("sec", "dp", "seq"), None, None),
        P(("sec", "dp", "seq"), None),
        P(("sec", "dp", "seq"), None),
        P(("sec", "dp", "seq"), None, None),
        P(("sec", "dp", "seq")),
        P(),
        P(),
        P(),
        P(None, None, "seq"),
        P("seq", None),
        P("seq", None),
        P(),
        P(("sec", "dp")),
        P(("sec", "dp")),
    )
    return jax.shard_map(
        local,
        mesh=mesh,
        in_specs=placed,
        out_specs=(P(("sec", "dp")), P("seq", None), P(("sec", "dp", "seq"), None, None)),
        check_vma=False,
    )
```

profile of v0, /device:TPU:2, one launch (start us, length us, event | category | flops | bytes accessed | tf_op | source)
XLA Modules:
  0.0 640.3 jit_solution(5430359469314224564)
XLA Ops:
  7.2 0.9 compare_and_fusion
  8.2 0.9 copy-done
  9.1 5.1 gather_fusion
  14.2 2.3 select_reduce_fusion
  17.3 1.3 convert_reduce_fusion
  18.5 1.4 fusion.22
  20.0 0.6 fusion.77
  20.7 1.8 fusion.24
  22.5 0.8 slice_reduce_fusion.1
  23.8 0.5 copy-done.33
  25.1 0.6 subtract_reduce_fusion.1
  26.0 1.7 multiply_reduce_fusion.3
  27.8 0.9 copy-done.4
  28.7 0.9 fusion.74
  29.8 0.5 neg.19
  30.3 88.0 %all-reduce.3.cloned.1.call-done = f32[32,512]{1,0:T(8,128)} async-done(((f32[32,512]{1,0:T(8,128)}), f32[32,512]{1,0:T(8,128)}) %all-reduce.3.cloned.1.call-update) | async-done | bytes 65552 | tf_op jit(solution)/shard_map/psum | solution.py:100
  118.3 1.0 multiply_reduce_fusion.8
  119.3 0.5 add_sqrt_fusion.2
  119.8 55.7 %all-gather.3.cloned.1.call-done = bf16[2048,2048]{1,0:T(8,128)(2,1)} async-done(((bf16[128,2048]{1,0:T(8,128)(2,1)}), bf16[2048,2048]{1,0:T(8,128)(2,1)}) %all-gather.3.cloned.1.call-update) | async-done | bytes 8388624 | tf_op jit(solution)/shard_map/all_gather | solution.py:115
  175.5 6.4 convolution_bitcast_fusion.1
  182.1 1.6 fusion.32
  183.9 2.7 convert_reduce_fusion.1
  186.6 2.1 fusion.37
  188.8 47.4 %psum.21 = f32[16,512]{1,0:T(8,128)} all-reduce(f32[16,512]{1,0:T(8,128)S(1)} %fusion.59), channel_id=1, replica_groups=mesh['sec'=2,'dp'=8,'seq'=16] {'seq'}, use_global_device_ids=true, to_apply=%region_10.11 | all-reduce | flops 8192 | bytes 65536 | tf_op jit(solution)/shard_map/psum | solution.py:139
  236.2 1.2 multiply_reduce_fusion.9
  237.5 1.0 fusion.45
  238.4 0.4 multiply_convert_fusion
  238.8 1.7 fusion.35
  241.0 0.6 convolution_bitcast_fusion.2
  241.5 1.0 copy-done.2
  242.7 0.8 multiply_reduce_fusion.1
  243.4 0.6 divide_convert_fusion.1
  244.0 0.8 copy-done.9
  244.8 8.1 %convolution_bitcast_fusion = f32[16,128,2048]{2,1,0:T(8,128)} fusion(bf16[16,128,1,128]{1,3,0,2:T(8,128)(2,1)S(1)} %multiply_convert_fusion, bf16[16,128,1,128]{1,3,0,2:T(8,128)(2,1)S(1)} %get-tuple-element.60, bf16[16,128,1,128]{1,3,0,2:T(8,128)(2,1)S(1)} %get-tuple-element.59, bf16[3,2048,128]{2,1,0:T(8,128)(2,1)S(1)} %copy-done.9), kind=kOutput, calls=%fused_computation.2 | convolution fusion | flops 3222798336 | bytes 19922944 | tf_op jit(solution)/shard_map/cfjk,jdk->cfd/dot_general | solution.py:182
  253.2 100.2 %reduce-scatter.2.cloned.1.call-done = f32[1,128,2048]{2,1,0:T(8,128)} async-done(((f32[16,128,2048]{2,1,0:T(8,128)}), f32[1,128,2048]{2,1,0:T(8,128)}) %reduce-scatter.2.cloned.1.call-update) | async-done | bytes 1048592 | tf_op jit(solution)/shard_map/reduce_scatter | solution.py:181
  353.5 1.9 fusion.30
  355.7 2.1 multiply_reduce_fusion.7
  358.4 2.0 fusion.66
  360.8 2.7 fusion.27
  363.6 1.3 fusion.40
  364.9 1.0 scatter-add.10
  367.2 3.3 fusion.53
  370.5 0.7 copy-done.15
  371.2 3.2 fusion.18
  374.3 1.5 reduce_sum.224
  375.8 2.8 fusion.21
  378.7 253.5 %all-reduce.5.cloned.1.call-done = f32[2560,256]{1,0:T(8,128)} async-done(((f32[2560,256]{1,0:T(8,128)}), f32[2560,256]{1,0:T(8,128)}) %all-reduce.5.cloned.1.call-update) | async-done | bytes 2621456 | tf_op jit(solution)/shard_map/psum | solution.py:201
  632.2 1.6 constant_dynamic-slice_fusion
  (110 shorter events, 5.8 us)
Async XLA Ops:
  7.2 1.9 copy-start
  7.2 111.1 %all-reduce.3.cloned.1.call-start = ((), (), s32[]{:S(2)}) async-start(), calls=%async_computation.1 | async-start | bytes 131072 | tf_op jit(solution)/shard_map/psum | solution.py:100
  14.1 5.8 copy-start.20
  14.1 6.4 %copy-start.21 = (bf16[1,2560]{1,0:T(2,128)(2,1)S(1)}, bf16[1,2560]{1,0:T(2,128)(2,1)}, u32[]{:S(2)}) copy-start(bf16[1,2560]{1,0:T(2,128)(2,1)} %param.21) | copy-start | bytes 15364
  14.1 6.4 %copy-start.22 = (bf16[1,2560]{1,0:T(2,128)(2,1)S(1)}, bf16[1,2560]{1,0:T(2,128)(2,1)}, u32[]{:S(2)}) copy-start(bf16[1,2560]{1,0:T(2,128)(2,1)} %param.22) | copy-start | bytes 15364
  14.2 6.5 %copy-start.36 = (bf16[1,128,256]{2,1,0:T(8,128)(2,1)S(1)}, bf16[1,128,256]{2,1,0:T(8,128)(2,1)}, u32[]{:S(2)}) copy-start(bf16[1,128,256]{2,1,0:T(8,128)(2,1)} %param.23) | copy-start | bytes 196612
  16.5 159.0 %all-gather.3.cloned.1.call-start = ((), (), s32[]{:S(2)}) async-start(), calls=%async_computation.4 | async-start | bytes 8912896 | tf_op jit(solution)/shard_map/all_gather | solution.py:115
  16.5 4.1 copy-start.3
  18.5 3.9 copy-start.23
  20.0 2.5 copy-start.27
  20.7 1.8 copy-start.14
  20.7 1.8 copy-start.17
  23.3 0.6 copy-start.31
  23.8 0.5 copy-start.33
  24.9 2.8 copy-start.10
  27.7 1.0 copy-start.4
  27.8 2.0 copy-start.37
  27.8 1.0 copy-start.25
  29.7 323.8 %reduce-scatter.2.cloned.1.call-start = ((), (), s32[]{:S(2)}) async-start(), calls=%async_computation.2 | async-start | bytes 17825792 | tf_op jit(solution)/shard_map/reduce_scatter | solution.py:181
  181.9 2.0 copy-start.1
  183.9 4.8 copy-start.13
  183.9 52.3 %copy-start.16 = (f32[32,512]{1,0:T(8,128)S(1)}, f32[32,512]{1,0:T(8,128)}, u32[]{:S(2)}) copy-start(f32[32,512]{1,0:T(8,128)} %all-reduce.3.cloned.1.call-done) | copy-start | bytes 196612
  236.2 4.4 copy-start.6
  237.4 3.5 copy-start.35
  238.4 2.5 copy-start.8
  240.6 1.9 copy-start.2
  241.0 1.7 copy-start.12
  243.4 1.4 copy-start.9
  253.0 100.5 %copy-start.26 = (f32[128]{0:T(128)S(1)}, f32[128]{0:T(128)}, u32[]{:S(2)}) copy-start(f32[128]{0:T(128)} %copy-done.25) | copy-start | bytes 1540
  253.0 102.5 %copy-start.19 = (f32[1,2048]{1,0:T(1,128)S(1)}, f32[1,2048]{1,0:T(1,128)}, u32[]{:S(2)}) copy-start(f32[1,2048]{1,0:T(1,128)} %get-tuple-element.67) | copy-start | bytes 24580
  253.0 102.5 %copy-start.18 = (f32[1,2048]{1,0:T(1,128)S(1)}, f32[1,2048]{1,0:T(1,128)}, u32[]{:S(2)}) copy-start(f32[1,2048]{1,0:T(1,128)} %get-tuple-element.66) | copy-start | bytes 24580
  253.0 379.2 %all-reduce.5.cloned.1.call-start = ((), (), s32[]{:S(2)}) async-start(), calls=%async_computation.3 | async-start | bytes 5242880 | tf_op jit(solution)/shard_map/psum | solution.py:201
  353.5 2.0 copy-start.5
  353.5 2.2 copy-start.7
  355.6 2.7 copy-start.29
  355.6 2.7 copy-start.30
  355.6 2.7 copy-start.32
  355.6 2.7 copy-start.34
  355.6 5.0 copy-start.11
  370.5 0.7 copy-start.15
  370.5 0.7 copy-start.24
  370.5 0.7 copy-start.28
Sparse Core Ops, SparseCore 0:
  16.6 101.6 all-reduce.2
  120.9 54.6 all-gather.2
  253.1 100.3 reduce-scatter.1
  370.6 261.4 all-reduce.4
where the time goes:
time: 641 us; the launch traced here: 640 us
  waiting for transfers between devices  498 us (78%)
  blocking collectives  47.4 us (7%)
  matrix products  37.3 us (6%)
  other arithmetic  26.9 us (4%)
  local copies, waits for them, and re-layouts  15.9 us (2%)
  between operations  14.9 us (2%)
    psum x1, waiting for transfers between devices, local(): grad_total = lax.psum(grad_term, ('sec', 'dp', 'seq'))  253 us
    reduce_scatter x1, waiting for transfers between devices, local(): lax.psum_scatter(jnp.einsum('cfjk,jdk->cfd', d_proj, w_qkv, preferred_ele...  100 us
    psum x1, waiting for transfers between devices, local(): text_raw = lax.psum(text_part, 'seq')  88 us
    all_gather x1, waiting for transfers between devices, local(): lax.all_gather(normed_e.astype(jnp.bfloat16), 'seq', axis=0, tiled=True)  55.7 us
    psum x1, blocking collectives, local(): motion_emb = lax.psum(motion_part, 'seq')  47.4 us
  transfers between devices with their start and end apart: 4, of which 4 were waited for; matrix products, arithmetic and copies ran while one was open for 3% of the time, Pallas kernels for 0%

commit v1 on v0

--- a/solution.py
+++ b/solution.py
@@ -9,6 +9,24 @@
 normalizing_sharpness = 10.0
 epsilon = 1e-06
 highest = lax.Precision.HIGHEST
+
+
+def gather_around(value, axis, dim):
+    ways, here, step = (lax.axis_size(axis), lax.axis_index(axis), value.shape[dim])
+    shape = [n * ways if d == dim else n for d, n in enumerate(value.shape)]
+    full = lax.dynamic_update_slice_in_dim(
+        jnp.zeros(shape, value.dtype), value, here * step, axis=dim
+    )
+    going_up = going_down = value
+    for far in range(1, ways // 2 + 1):
+        going_up = lax.ppermute(going_up, axis, [(d, (d + 1) % ways) for d in range(ways)])
+        full = lax.dynamic_update_slice_in_dim(full, going_up, (here - far) % ways * step, axis=dim)
+        if 2 * far < ways:
+            going_down = lax.ppermute(going_down, axis, [(d, (d - 1) % ways) for d in range(ways)])
+            full = lax.dynamic_update_slice_in_dim(
+                full, going_down, (here + far) % ways * step, axis=dim
+            )
+    return full
 
 
 def rotate(angle, first, second):
@@ -112,7 +130,7 @@
     normed_e, scale_rms = embed(x_clean, path_east, path_north, w_embed, root_rows)
     projected = jnp.einsum(
         "cfd,jdk->cfjk",
-        lax.all_gather(normed_e.astype(jnp.bfloat16), "seq", axis=0, tiled=True),
+        gather_around(normed_e.astype(jnp.bfloat16), "seq", 0),
         w_qkv,
         preferred_element_type=jnp.float32,
     )

time: 641 us -> 670 us (1.045)
  starting transfers between devices: 0.34 us -> 23.5 us
  local copies, waits for them, and re-layouts: 15.9 us -> 36.4 us
  waiting for transfers between devices: 498 us -> 482 us
    all_gather x1 -> x0, waiting for transfers between devices: 55.7 us -> none  [local(): lax.all_gather(normed_e.astype(jnp.bfloat16), 'seq', axis=0, tiled=True)]
    ppermute x0 -> x15, waiting for transfers between devices: none -> 32.7 us  [the longest x8 27.9 us: gather_around(): lax.ppermute(going_up, axis, [(d, (d + 1) % ways) for d in range(ways)])]
    ppermute x0 -> x15, starting transfers between devices: none -> 23.4 us  [the longest x7 22.9 us: gather_around(): lax.ppermute(going_down, axis, [(d, (d - 1) % ways) for d in range(ways)])]
    dynamic_update_slice x0 -> x15, local copies, waits for them, and re-layouts: none -> 18.9 us  [the longest x8 9.89 us: gather_around(): lax.dynamic_update_slice_in_dim(full, going_up, (here - far) % ways * ste...]
    psum x1, waiting for transfers between devices: 88 us -> 96 us  [local(): text_raw = lax.psum(text_part, 'seq')]
  transfers between devices with their start and end apart: 4 -> 18, of which waited for: 4 -> 13; matrix products, arithmetic and copies ran while one was open for 3% -> 5% of each run, Pallas kernels for 0% -> 0%
where the time goes in v1:
time: 670 us; the launch traced here: 668 us
  waiting for transfers between devices  482 us (72%)
  blocking collectives  46.5 us (7%)
  matrix products  38.1 us (6%)
  local copies, waits for them, and re-layouts  36.4 us (5%)
  other arithmetic  26.8 us (4%)
  starting transfers between devices  23.5 us (4%)
  between operations  15.2 us (2%)
    psum x1, waiting for transfers between devices, local(): grad_total = lax.psum(grad_term, ('sec', 'dp', 'seq'))  254 us
    reduce_scatter x1, waiting for transfers between devices, local(): lax.psum_scatter(jnp.einsum('cfjk,jdk->cfd', d_proj, w_qkv, preferred_ele...  99.1 us
    psum x1, waiting for transfers between devices, local(): text_raw = lax.psum(text_part, 'seq')  96 us
    psum x1, blocking collectives, local(): motion_emb = lax.psum(motion_part, 'seq')  46.5 us
    ppermute x8, waiting for transfers between devices, gather_around(): lax.ppermute(going_up, axis, [(d, (d + 1) % ways) for d in range(ways)])  27.9 us
    ppermute x7, starting transfers between devices, gather_around(): lax.ppermute(going_down, axis, [(d, (d - 1) % ways) for d in range(ways)])  22.9 us
  transfers between devices with their start and end apart: 18, of which 13 were waited for; matrix products, arithmetic and copies ran while one was open for 5% of the time, Pallas kernels for 0%

profile of v1, /device:TPU:2, one launch (start us, length us, event | category | flops | bytes accessed | tf_op | source)
XLA Modules:
  0.0 668.5 jit_solution(13290236403225343962)
XLA Ops:
  7.2 1.4 convert_reduce_fusion
  8.7 1.4 fusion.27
  12.1 1.9 fusion.29
  18.4 2.6 multiply_reduce_fusion.3
  23.2 3.2 copy-done.5
  26.4 5.3 collective-permute-start.1
  31.7 7.2 %collective-permute-done = bf16[1,128,2048]{2,1,0:T(8,128)(2,1)} collective-permute-done((bf16[1,128,2048]{2,1,0:T(8,128)(2,1)}, bf16[1,128,2048]{2,1,0:T(8,128)(2,1)}, u32[]{:S(2)}, u32[]{:S(2)}) %collective-permute-start) | collective-permute-done | bytes 524320 | tf_op jit(solution)/shard_map/ppermute | solution.py:22
  38.9 3.0 collective-permute-start.3
  42.0 7.1 %collective-permute-done.2 = bf16[1,128,2048]{2,1,0:T(8,128)(2,1)} collective-permute-done((bf16[1,128,2048]{2,1,0:T(8,128)(2,1)}, bf16[1,128,2048]{2,1,0:T(8,128)(2,1)}, u32[]{:S(2)}, u32[]{:S(2)}) %collective-permute-start.2) | collective-permute-done | bytes 524320 | tf_op jit(solution)/shard_map/ppermute | solution.py:22
  49.1 5.1 gather_fusion
  54.1 2.2 select_reduce_fusion
  57.2 2.9 collective-permute-start.5
  60.2 96.0 %all-reduce.3.cloned.1.call-done = f32[32,512]{1,0:T(8,128)} async-done(((f32[32,512]{1,0:T(8,128)}), f32[32,512]{1,0:T(8,128)}) %all-reduce.3.cloned.1.call-update) | async-done | bytes 65552 | tf_op jit(solution)/shard_map/psum | solution.py:118
  158.1 1.9 constant_dynamic-update-slice_fusion.14
  160.0 2.5 collective-permute-start.7
  162.6 1.9 constant_dynamic-update-slice_fusion.13
  164.5 2.8 collective-permute-done.6
  167.2 1.9 constant_dynamic-update-slice_fusion.12
  169.1 1.9 constant_dynamic-update-slice_fusion.11
  171.0 3.0 collective-permute-start.9
  174.0 1.9 constant_dynamic-update-slice_fusion.10
  177.1 1.9 constant_dynamic-update-slice_fusion.9
  180.7 3.1 collective-permute-start.11
  184.6 2.2 collective-permute-done.10
  188.6 1.9 collective-permute-done.11
  190.5 3.1 collective-permute-start.13
  194.5 2.2 collective-permute-done.12
  198.4 2.0 collective-permute-done.13
  201.2 5.3 collective-permute-done.14
  207.3 5.9 fusion.4
  213.5 1.6 fusion.37
  215.3 2.7 convert_reduce_fusion.1
  217.9 2.1 fusion.42
  220.2 46.5 %psum.21 = f32[16,512]{1,0:T(8,128)} all-reduce(f32[16,512]{1,0:T(8,128)S(1)} %fusion.64), channel_id=1, replica_groups=mesh['sec'=2,'dp'=8,'seq'=16] {'seq'}, use_global_device_ids=true, to_apply=%region_10.11 | all-reduce | flops 8192 | bytes 65536 | tf_op jit(solution)/shard_map/psum | solution.py:157
  269.4 1.9 fusion.40
  274.4 8.1 %convolution_bitcast_fusion = f32[16,128,2048]{2,1,0:T(8,128)} fusion(bf16[16,128,1,128]{1,3,0,2:T(8,128)(2,1)S(1)} %multiply_convert_fusion, bf16[16,128,1,128]{1,3,0,2:T(8,128)(2,1)S(1)} %get-tuple-element.62, bf16[16,128,1,128]{1,3,0,2:T(8,128)(2,1)S(1)} %get-tuple-element.61, bf16[3,2048,128]{2,1,0:T(8,128)(2,1)S(1)} %copy-done.10), kind=kOutput, calls=%fused_computation.4 | convolution fusion | flops 3222798336 | bytes 19922944 | tf_op jit(solution)/shard_map/cfjk,jdk->cfd/dot_general | solution.py:200
  282.7 99.1 %reduce-scatter.2.cloned.1.call-done = f32[1,128,2048]{2,1,0:T(8,128)} async-done(((f32[16,128,2048]{2,1,0:T(8,128)}), f32[1,128,2048]{2,1,0:T(8,128)}) %reduce-scatter.2.cloned.1.call-update) | async-done | bytes 1048592 | tf_op jit(solution)/shard_map/reduce_scatter | solution.py:199
  381.8 1.9 fusion.35
  383.9 2.1 multiply_reduce_fusion.7
  386.7 2.0 fusion.71
  389.1 2.7 fusion.32
  391.8 1.3 fusion.45
  395.5 3.3 fusion.58
  398.8 3.2 fusion.23
  402.0 1.5 reduce_sum.224
  403.4 2.8 fusion.26
  406.3 254.1 %all-reduce.5.cloned.1.call-done = f32[2560,256]{1,0:T(8,128)} async-done(((f32[2560,256]{1,0:T(8,128)}), f32[2560,256]{1,0:T(8,128)}) %all-reduce.5.cloned.1.call-update) | async-done | bytes 2621456 | tf_op jit(solution)/shard_map/psum | solution.py:219
  660.4 1.6 constant_dynamic-slice_fusion
  (153 shorter events, 29.9 us)
Async XLA Ops:
  7.2 41.9 %copy-start = (bf16[3088,512]{1,0:T(8,128)(2,1)S(1)}, bf16[3088,512]{1,0:T(8,128)(2,1)}, u32[]{:S(2)}) copy-start(bf16[3088,512]{1,0:T(8,128)(2,1)} %param.30) | copy-start | bytes 9486340
  7.2 149.1 %all-reduce.3.cloned.1.call-start = ((), (), s32[]{:S(2)}) async-start(), calls=%async_computation.1 | async-start | bytes 131072 | tf_op jit(solution)/shard_map/psum | solution.py:118
  8.6 6.2 copy-start.24
  10.1 4.8 copy-start.28
  11.5 2.5 copy-start.18
  16.5 5.6 copy-start.11
  18.4 3.7 copy-start.19
  18.4 3.7 copy-start.21
  21.0 20.8 %copy-start.23 = (s32[32,32]{1,0:T(8,128)S(1)}, s32[32,32]{1,0:T(8,128)}, u32[]{:S(2)}) copy-start(s32[32,32]{1,0:T(8,128)} %param.31) | copy-start | bytes 12292
  23.2 3.2 copy-start.5
  26.4 12.5 %collective-permute-start = (bf16[1,128,2048]{2,1,0:T(8,128)(2,1)}, bf16[1,128,2048]{2,1,0:T(8,128)(2,1)}, u32[]{:S(2)}, u32[]{:S(2)}) collective-permute-start(bf16[1,128,2048]{2,1,0:T(8,128)(2,1)} %get-tuple-element.58), channel_id=1, source_target_pairs={{0,1},{1,2},{2,3},{3,4},{4,5},{5,6},{6,7},{7,8},{8,9},{9,10},{10,1... | collective-permute-start | bytes 1572872 | tf_op jit(solution)/shard_map/ppermute | solution.py:22
  26.4 12.5 %collective-permute-start.1 = (bf16[1,128,2048]{2,1,0:T(8,128)(2,1)}, bf16[1,128,2048]{2,1,0:T(8,128)(2,1)}, u32[]{:S(2)}, u32[]{:S(2)}) collective-permute-start(bf16[1,128,2048]{2,1,0:T(8,128)(2,1)} %get-tuple-element.58), channel_id=1, source_target_pairs={{0,15},{1,0},{2,1},{3,2},{4,3},{5,4},{6,5},{7,6},{8,7},{9,8},{10,9... | collective-permute-start | bytes 1572872 | tf_op jit(solution)/shard_map/ppermute | solution.py:25
  38.9 10.1 %collective-permute-start.2 = (bf16[1,128,2048]{2,1,0:T(8,128)(2,1)}, bf16[1,128,2048]{2,1,0:T(8,128)(2,1)}, u32[]{:S(2)}, u32[]{:S(2)}) collective-permute-start(bf16[1,128,2048]{2,1,0:T(8,128)(2,1)} %collective-permute-done), channel_id=1, source_target_pairs={{0,1},{1,2},{2,3},{3,4},{4,5},{5,6},{6,7},{7,8},{8,9},{9,10},{10,1... | collective-permute-start | bytes 1572872 | tf_op jit(solution)/shard_map/ppermute | solution.py:22
  38.9 18.3 %collective-permute-start.3 = (bf16[1,128,2048]{2,1,0:T(8,128)(2,1)}, bf16[1,128,2048]{2,1,0:T(8,128)(2,1)}, u32[]{:S(2)}, u32[]{:S(2)}) collective-permute-start(bf16[1,128,2048]{2,1,0:T(8,128)(2,1)} %collective-permute-done.1), channel_id=1, source_target_pairs={{0,15},{1,0},{2,1},{3,2},{4,3},{5,4},{6,5},{7,6},{8,7},{9,8},{10,9... | collective-permute-start | bytes 1572872 | tf_op jit(solution)/shard_map/ppermute | solution.py:25
  49.0 108.1 %collective-permute-start.4 = (bf16[1,128,2048]{2,1,0:T(8,128)(2,1)}, bf16[1,128,2048]{2,1,0:T(8,128)(2,1)}, u32[]{:S(2)}, u32[]{:S(2)}) collective-permute-start(bf16[1,128,2048]{2,1,0:T(8,128)(2,1)} %collective-permute-done.2), channel_id=1, source_target_pairs={{0,1},{1,2},{2,3},{3,4},{4,5},{5,6},{6,7},{7,8},{8,9},{9,10},{10,1... | collective-permute-start | bytes 1572872 | tf_op jit(solution)/shard_map/ppermute | solution.py:22
  49.1 7.6 %copy-start.37 = (f32[16]{0:T(128)S(1)}, f32[16]{0:T(128)}, u32[]{:S(2)}) copy-start(f32[16]{0:T(128)} %param.33) | copy-start | bytes 196
  56.4 325.3 %reduce-scatter.2.cloned.1.call-start = ((), (), s32[]{:S(2)}) async-start(), calls=%async_computation.2 | async-start | bytes 17825792 | tf_op jit(solution)/shard_map/reduce_scatter | solution.py:199
  57.2 102.8 %collective-permute-start.5 = (bf16[1,128,2048]{2,1,0:T(8,128)(2,1)}, bf16[1,128,2048]{2,1,0:T(8,128)(2,1)}, u32[]{:S(2)}, u32[]{:S(2)}) collective-permute-start(bf16[1,128,2048]{2,1,0:T(8,128)(2,1)} %collective-permute-done.3), channel_id=1, source_target_pairs={{0,15},{1,0},{2,1},{3,2},{4,3},{5,4},{6,5},{7,6},{8,7},{9,8},{10,9... | collective-permute-start | bytes 1572872 | tf_op jit(solution)/shard_map/ppermute | solution.py:25
  157.2 10.0 %collective-permute-start.6 = (bf16[1,128,2048]{2,1,0:T(8,128)(2,1)}, bf16[1,128,2048]{2,1,0:T(8,128)(2,1)S(1)}, u32[]{:S(2)}, u32[]{:S(2)}) collective-permute-start(bf16[1,128,2048]{2,1,0:T(8,128)(2,1)} %collective-permute-done.4), channel_id=1, source_target_pairs={{0,1},{1,2},{2,3},{3,4},{4,5},{5,6},{6,7},{7,8},{8,9},{9,10},{10,1... | collective-permute-start | bytes 1572872 | tf_op jit(solution)/shard_map/ppermute | solution.py:22
  160.0 11.0 %collective-permute-start.7 = (bf16[1,128,2048]{2,1,0:T(8,128)(2,1)}, bf16[1,128,2048]{2,1,0:T(8,128)(2,1)S(1)}, u32[]{:S(2)}, u32[]{:S(2)}) collective-permute-start(bf16[1,128,2048]{2,1,0:T(8,128)(2,1)} %collective-permute-done.5), channel_id=1, source_target_pairs={{0,15},{1,0},{2,1},{3,2},{4,3},{5,4},{6,5},{7,6},{8,7},{9,8},{10,9... | collective-permute-start | bytes 1572872 | tf_op jit(solution)/shard_map/ppermute | solution.py:25
  167.2 9.8 %collective-permute-start.8 = (bf16[1,128,2048]{2,1,0:T(8,128)(2,1)S(1)}, bf16[1,128,2048]{2,1,0:T(8,128)(2,1)S(1)}, u32[]{:S(2)}, u32[]{:S(2)}) collective-permute-start(bf16[1,128,2048]{2,1,0:T(8,128)(2,1)S(1)} %collective-permute-done.6), channel_id=1, source_target_pairs={{0,1},{1,2},{2,3},{3,4},{4,5},{5,6},{6,7},{7,8},{8,9},{9,10},{10,1... | collective-permute-start | bytes 1572872 | tf_op jit(solution)/shard_map/ppermute | solution.py:22
  171.0 9.7 %collective-permute-start.9 = (bf16[1,128,2048]{2,1,0:T(8,128)(2,1)S(1)}, bf16[1,128,2048]{2,1,0:T(8,128)(2,1)S(1)}, u32[]{:S(2)}, u32[]{:S(2)}) collective-permute-start(bf16[1,128,2048]{2,1,0:T(8,128)(2,1)S(1)} %collective-permute-done.7), channel_id=1, source_target_pairs={{0,15},{1,0},{2,1},{3,2},{4,3},{5,4},{6,5},{7,6},{8,7},{9,8},{10,9... | collective-permute-start | bytes 1572872 | tf_op jit(solution)/shard_map/ppermute | solution.py:25
  177.0 9.8 %collective-permute-start.10 = (bf16[1,128,2048]{2,1,0:T(8,128)(2,1)S(1)}, bf16[1,128,2048]{2,1,0:T(8,128)(2,1)S(1)}, u32[]{:S(2)}, u32[]{:S(2)}) collective-permute-start(bf16[1,128,2048]{2,1,0:T(8,128)(2,1)S(1)} %collective-permute-done.8), channel_id=1, source_target_pairs={{0,1},{1,2},{2,3},{3,4},{4,5},{5,6},{6,7},{7,8},{8,9},{9,10},{10,1... | collective-permute-start | bytes 1572872 | tf_op jit(solution)/shard_map/ppermute | solution.py:22
  180.7 9.8 %collective-permute-start.11 = (bf16[1,128,2048]{2,1,0:T(8,128)(2,1)S(1)}, bf16[1,128,2048]{2,1,0:T(8,128)(2,1)S(1)}, u32[]{:S(2)}, u32[]{:S(2)}) collective-permute-start(bf16[1,128,2048]{2,1,0:T(8,128)(2,1)S(1)} %collective-permute-done.9), channel_id=1, source_target_pairs={{0,15},{1,0},{2,1},{3,2},{4,3},{5,4},{6,5},{7,6},{8,7},{9,8},{10,9... | collective-permute-start | bytes 1572872 | tf_op jit(solution)/shard_map/ppermute | solution.py:25
  186.9 9.8 %collective-permute-start.12 = (bf16[1,128,2048]{2,1,0:T(8,128)(2,1)S(1)}, bf16[1,128,2048]{2,1,0:T(8,128)(2,1)S(1)}, u32[]{:S(2)}, u32[]{:S(2)}) collective-permute-start(bf16[1,128,2048]{2,1,0:T(8,128)(2,1)S(1)} %collective-permute-done.10), channel_id=1, source_target_pairs={{0,1},{1,2},{2,3},{3,4},{4,5},{5,6},{6,7},{7,8},{8,9},{9,10},{10,1... | collective-permute-start | bytes 1572872 | tf_op jit(solution)/shard_map/ppermute | solution.py:22
  188.6 18.8 %copy-start.9 = (bf16[3,2048,128]{2,1,0:T(8,128)(2,1)S(1)}, bf16[3,2048,128]{2,1,0:T(8,128)(2,1)}, u32[]{:S(2)}) copy-start(bf16[3,2048,128]{2,1,0:T(8,128)(2,1)} %param.28) | copy-start | bytes 4718596
  190.5 9.8 %collective-permute-start.13 = (bf16[1,128,2048]{2,1,0:T(8,128)(2,1)S(1)}, bf16[1,128,2048]{2,1,0:T(8,128)(2,1)S(1)}, u32[]{:S(2)}, u32[]{:S(2)}) collective-permute-start(bf16[1,128,2048]{2,1,0:T(8,128)(2,1)S(1)} %collective-permute-done.11), channel_id=1, source_target_pairs={{0,15},{1,0},{2,1},{3,2},{4,3},{5,4},{6,5},{7,6},{8,7},{9,8},{10,9... | collective-permute-start | bytes 1572872 | tf_op jit(solution)/shard_map/ppermute | solution.py:25
  196.7 9.8 %collective-permute-start.14 = (bf16[1,128,2048]{2,1,0:T(8,128)(2,1)S(1)}, bf16[1,128,2048]{2,1,0:T(8,128)(2,1)S(1)}, u32[]{:S(2)}, u32[]{:S(2)}) collective-permute-start(bf16[1,128,2048]{2,1,0:T(8,128)(2,1)S(1)} %collective-permute-done.12), channel_id=1, source_target_pairs={{0,1},{1,2},{2,3},{3,4},{4,5},{5,6},{6,7},{7,8},{8,9},{9,10},{10,1... | collective-permute-start | bytes 1572872 | tf_op jit(solution)/shard_map/ppermute | solution.py:22
  215.3 4.8 copy-start.14
  215.3 51.4 %copy-start.17 = (f32[32,512]{1,0:T(8,128)S(1)}, f32[32,512]{1,0:T(8,128)}, u32[]{:S(2)}) copy-start(f32[32,512]{1,0:T(8,128)} %all-reduce.3.cloned.1.call-done) | copy-start | bytes 196612
  266.7 4.6 copy-start.6
  266.7 4.9 copy-start.8
  268.0 4.2 copy-start.36
  269.0 3.3 copy-start.2
  269.0 3.3 copy-start.13
  282.6 99.2 %copy-start.27 = (f32[128]{0:T(128)S(1)}, f32[128]{0:T(128)}, u32[]{:S(2)}) copy-start(f32[128]{0:T(128)} %copy-done.26) | copy-start | bytes 1540
  282.6 101.2 %copy-start.20 = (f32[1,2048]{1,0:T(1,128)S(1)}, f32[1,2048]{1,0:T(1,128)}, u32[]{:S(2)}) copy-start(f32[1,2048]{1,0:T(1,128)} %copy-done.19) | copy-start | bytes 24580
  282.6 101.2 %copy-start.22 = (f32[1,2048]{1,0:T(1,128)S(1)}, f32[1,2048]{1,0:T(1,128)}, u32[]{:S(2)}) copy-start(f32[1,2048]{1,0:T(1,128)} %copy-done.21) | copy-start | bytes 24580
  282.6 377.8 %all-reduce.5.cloned.1.call-start = ((), (), s32[]{:S(2)}) async-start(), calls=%async_computation.3 | async-start | bytes 5242880 | tf_op jit(solution)/shard_map/psum | solution.py:219
  282.6 104.0 %copy-start.30 = (f32[128]{0:T(128)S(1)}, f32[128]{0:T(128)}, u32[]{:S(2)}) copy-start(f32[128]{0:T(128)} %get-tuple-element.49) | copy-start | bytes 1540
  282.6 104.0 %copy-start.31 = (f32[128]{0:T(128)S(1)}, f32[128]{0:T(128)}, u32[]{:S(2)}) copy-start(f32[128]{0:T(128)} %get-tuple-element.50) | copy-start | bytes 1540
  282.7 104.0 %copy-start.33 = (f32[128]{0:T(128)S(1)}, f32[128]{0:T(128)}, u32[]{:S(2)}) copy-start(f32[128]{0:T(128)} %copy-done.32) | copy-start | bytes 1540
  282.7 104.0 %copy-start.35 = (f32[1,128]{1,0:T(1,128)S(1)}, f32[1,128]{1,0:T(1,128)}, u32[]{:S(2)}) copy-start(f32[1,128]{1,0:T(1,128)} %copy-done.34) | copy-start | bytes 1540
  381.8 2.2 copy-start.7
  381.8 7.2 %copy-start.12 = (f32[1,128,1]{2,1,0:T(8,128)S(1)}, f32[1,128,1]{2,1,0:T(8,128)}, u32[]{:S(2)}) copy-start(f32[1,128,1]{2,1,0:T(8,128)} %copy-done.11) | copy-start | bytes 1540
  395.5 3.3 copy-start.16
  395.5 3.3 copy-start.25
  395.5 3.3 copy-start.29
  (8 other events, 9.4 us)
Sparse Core Ops, SparseCore 0:
  56.5 99.6 all-reduce.2
  282.7 98.9 reduce-scatter.1
  398.9 261.4 all-reduce.4
